TPU v7x, 128 devices: a whole 4x4x4 slice. The times are simulated.
128 devices in a mesh: seq: 16 (over x_hi, z, core), tp: 8 (over y, x_lo).
Axes of the slice: x: 4 (x_hi: 2, x_lo: 2; x = x_hi * 2 + x_lo), y: 4, z: 4, core: 2. Of those that a mesh axis runs over, the one named last changes fastest.
Arguments:
- tokens: bfloat16 [4, 2048, 4096], P(None, 'seq', 'tp'), may hold values from -6 to 6
- new_tokens: bfloat16 [4, 4096], P(None, 'tp'), may hold values from -6 to 6
- w_qkv: bfloat16 [3, 4096, 4096], P(None, None, 'tp')
- w_out: bfloat16 [4096, 4096], P('tp')
- q_gain: float32 [4096], P('tp'), may hold values from 0.5 to 6
- k_gain: float32 [4096], P('tp'), may hold values from 0.5 to 6
- post_gain: float32 [4096], P('tp'), may hold values from 0.5 to 1.5
- lengths: int32 [4], replicated, may hold values from 1 to 2048, 6144 in all
Outputs:
- hidden_out: bfloat16 [4, 2048, 4096], P(None, 'seq', 'tp')
- new_out: bfloat16 [4, 4096], P(None, 'tp')
Inputs may be any that keep to these rules, and one draw needn't show every extreme that they name: `lengths`: one prompt has exactly 2048 live tokens.
All inputs are finite; a program needn't handle non-finite values.
Results may differ from a plain program's by a relative error of at most 0.012.
The roundings to bfloat16 on the way count: a program that leaves them out, or rounds other values in their place, can miss the bound.
Values may be sent and summed in bfloat16 or wider, within the bound.
No kernel may reach another device: no remote copies, remote signals or barrier semaphores. Data moves between devices by JAX's collectives and lax.ppermute only.
A program may use at most 128 MiB of HBM per device.

v0:
```python
from functools import partial
import jax
import jax.numpy as jnp
from jax import lax
from jax.sharding import PartitionSpec as P

HD = 128
rope_base = 500000.0
norm_eps = 1e-06
masked_fill = -1e30


def joined(value, axis, combine):
    everything = jax.tree.map(lambda part: lax.all_gather(part, axis), value)
    initial = jax.tree.map(lambda part: part[0], everything)

    def hop(k, so_far):
        return combine(so_far, jax.tree.map(lambda part: part[k], everything))

    return lax.fori_loop(1, lax.axis_size(axis), hop, initial)


def rotate(values, position):
    half = values.shape[-1] // 2
    freq = rope_base ** (-(jnp.arange(half, dtype=jnp.float32) * 2.0) / values.shape[-1])
    angle = position.astype(jnp.float32)[..., None] * freq
    cosine = jnp.cos(angle)
    sine = jnp.sin(angle)
    lower = values[..., :half]
    upper = values[..., half:]
    return jnp.concatenate([lower * cosine - upper * sine, upper * cosine + lower * sine], -1)


def fold_step(carry, pieces, start, queries, query_pos, lengths, scale):
    running_max, running_sum, running_acc = carry
    key_piece, value_piece = pieces
    count = key_piece.shape[1]
    scores = (
        jnp.einsum("sphe,snhe->shpn", queries, key_piece, preferred_element_type=jnp.float32)
        * scale
    )
    key_pos = jnp.arange(count, dtype=jnp.int32)
    valid = (key_pos[None, None, :] <= query_pos[None, :, None]) & (
        key_pos[None, None, :] < lengths[:, None, None]
    )
    valid = valid[:, None, :, :]
    scores = jnp.where(valid, scores, masked_fill)
    new_max = jnp.maximum(running_max, jnp.max(scores, -1))
    weights = jnp.where(valid, jnp.exp(scores - new_max[..., None]), 0.0)
    running_sum = jnp.sum(weights, -1)
    running_acc = jnp.einsum(
        "shpn,snhe->shpe",
        weights.astype(jnp.bfloat16),
        value_piece,
        preferred_element_type=jnp.float32,
    )
    return (new_max, running_sum, running_acc)


def combine(first, second):
    first_max, first_sum, first_acc = first
    second_max, second_sum, second_acc = second
    top = jnp.maximum(first_max, second_max)
    first_factor = jnp.exp(first_max - top)
    second_factor = jnp.exp(second_max - top)
    return (
        top,
        first_sum * first_factor + second_sum * second_factor,
        first_acc * first_factor[..., None] + second_acc * second_factor[..., None],
    )


def body(tokens, new_tokens, w_qkv, w_out, q_gain, k_gain, post_gain, lengths):
    seqs, pos_dev, width_local = tokens.shape
    heads_local = width_local // HD
    full_width = w_qkv.shape[1]
    prompt_rows = seqs * pos_dev
    flat_rows = tokens.reshape(prompt_rows, width_local)
    row_piece = lax.all_gather(flat_rows, "tp", axis=1, tiled=True)
    new_piece = lax.all_gather(new_tokens, "tp", axis=1, tiled=True)
    proj_rows = jnp.einsum("tn,cnf->ctf", row_piece, w_qkv, preferred_element_type=jnp.float32)
    proj_new = jnp.einsum("tn,cnf->ctf", new_piece, w_qkv, preferred_element_type=jnp.float32)
    query_rows, key_rows = (proj_rows[0], proj_rows[1])
    query_fresh, key_fresh = (proj_new[0], proj_new[1])
    query_sq, key_sq, query_new_sq, key_new_sq = lax.psum(
        (
            jnp.sum(query_rows * query_rows, -1),
            jnp.sum(key_rows * key_rows, -1),
            jnp.sum(query_fresh * query_fresh, -1),
            jnp.sum(key_fresh * key_fresh, -1),
        ),
        "tp",
    )

    def normed(values, square_sum, gain):
        return values * lax.rsqrt(square_sum[:, None] / full_width + norm_eps) * gain

    seq_index = lax.axis_index("seq")
    query_pos = seq_index * pos_dev + jnp.arange(pos_dev, dtype=jnp.int32)
    row_pos = jnp.tile(query_pos, seqs)
    queries = rotate(
        normed(query_rows, query_sq, q_gain).reshape(prompt_rows, heads_local, HD), row_pos[:, None]
    )
    queries = queries.astype(jnp.bfloat16).reshape(seqs, pos_dev, heads_local, HD)
    keys = rotate(
        normed(key_rows, key_sq, k_gain).reshape(prompt_rows, heads_local, HD), row_pos[:, None]
    )
    keys = keys.astype(jnp.bfloat16).reshape(seqs, pos_dev, heads_local, HD)
    values = proj_rows[2].astype(jnp.bfloat16).reshape(seqs, pos_dev, heads_local, HD)
    new_queries = rotate(
        normed(query_fresh, query_new_sq, q_gain).reshape(seqs, heads_local, HD), lengths[:, None]
    ).astype(jnp.bfloat16)
    new_keys = rotate(
        normed(key_fresh, key_new_sq, k_gain).reshape(seqs, heads_local, HD), lengths[:, None]
    ).astype(jnp.bfloat16)
    new_values = proj_new[2].astype(jnp.bfloat16).reshape(seqs, heads_local, HD)
    scale = HD ** (-0.5)
    start_carry = (
        jnp.full((seqs, heads_local, pos_dev), masked_fill, jnp.float32),
        jnp.zeros((seqs, heads_local, pos_dev), jnp.float32),
        jnp.zeros((seqs, heads_local, pos_dev, HD), jnp.float32),
    )
    stepper = partial(fold_step, queries=queries, query_pos=query_pos, lengths=lengths, scale=scale)
    final_max, final_sum, final_acc = stepper(
        start_carry,
        (
            lax.all_gather(keys, "seq", axis=1, tiled=True),
            lax.all_gather(values, "seq", axis=1, tiled=True),
        ),
        jnp.int32(0),
    )
    attention = (
        (final_acc / final_sum[..., None])
        .transpose(0, 2, 1, 3)
        .reshape(prompt_rows, width_local)
        .astype(jnp.bfloat16)
    )
    local_scores = (
        jnp.einsum("she,sphe->shp", new_queries, keys, preferred_element_type=jnp.float32) * scale
    )
    live = (query_pos[None, :] < lengths[:, None])[:, None, :]
    local_scores = jnp.where(live, local_scores, masked_fill)
    local_max = jnp.max(local_scores, -1)
    local_weights = jnp.where(live, jnp.exp(local_scores - local_max[..., None]), 0.0)
    local_sum = jnp.sum(local_weights, -1)
    local_acc = jnp.einsum(
        "shp,sphe->she",
        local_weights.astype(jnp.bfloat16),
        values,
        preferred_element_type=jnp.float32,
    )
    merged_max, merged_sum, merged_acc = joined((local_max, local_sum, local_acc), "seq", combine)
    self_score = (
        jnp.einsum("she,she->sh", new_queries, new_keys, preferred_element_type=jnp.float32) * scale
    )
    new_top = jnp.maximum(merged_max, self_score)
    keep_factor = jnp.exp(merged_max - new_top)
    own_weight = jnp.exp(self_score - new_top)
    new_total = merged_sum * keep_factor + own_weight
    own_rounded = lax.optimization_barrier(own_weight.astype(jnp.bfloat16)).astype(jnp.float32)
    numer = merged_acc * keep_factor[..., None] + own_rounded[..., None] * new_values.astype(
        jnp.float32
    )
    new_attention = (numer / new_total[..., None]).reshape(seqs, width_local).astype(jnp.bfloat16)
    part_rows = jnp.dot(attention, w_out, preferred_element_type=jnp.float32)
    part_new = jnp.dot(new_attention, w_out, preferred_element_type=jnp.float32)
    sum_rows, sum_new = (
        lax.psum(part_rows.astype(jnp.bfloat16), "tp").astype(jnp.float32),
        lax.psum(part_new.astype(jnp.bfloat16), "tp").astype(jnp.float32),
    )
    mean_rows = jnp.mean(sum_rows * sum_rows, -1)
    mean_new = jnp.mean(sum_new * sum_new, -1)
    offset = lax.axis_index("tp") * width_local
    own_rows = lax.dynamic_slice_in_dim(sum_rows, offset, width_local, 1)
    own_new = lax.dynamic_slice_in_dim(sum_new, offset, width_local, 1)
    out_rows = (
        flat_rows.astype(jnp.float32)
        + own_rows * lax.rsqrt(mean_rows[:, None] + norm_eps) * post_gain
    )
    out_new = (
        new_tokens.astype(jnp.float32)
        + own_new * lax.rsqrt(mean_new[:, None] + norm_eps) * post_gain
    )
    return (
        out_rows.astype(jnp.bfloat16).reshape(seqs, pos_dev, width_local),
        out_new.astype(jnp.bfloat16),
    )


def solution(mesh):
    in_specs = (
        P(None, "seq", "tp"),
        P(None, "tp"),
        P(None, None, "tp"),
        P("tp", None),
        P("tp"),
        P("tp"),
        P("tp"),
        P(),
    )
    out_specs = (P(None, "seq", "tp"), P(None, "tp"))
    return jax.shard_map(body, mesh=mesh, in_specs=in_specs, out_specs=out_specs, check_vma=False)
```

profile of v0, /device:TPU:1, one launch (start us, length us, event | category | flops | bytes accessed | tf_op | source)
XLA Modules:
  0.0 495.8 jit_solution(5832578119530907273)
XLA Ops:
  7.2 0.7 all-gather.9.cloned.1.call-update
  7.9 23.3 %all_gather.33 = bf16[4,4096]{1,0:T(4,128)(2,1)S(1)} all-gather(bf16[4,512]{1,0:T(4,128)(2,1)} %param.11), channel_id=1, replica_groups=mesh['seq'=16,'tp'=8] {'tp'}, dimensions={1}, use_global_device_ids=true | all-gather | bytes 36864 | tf_op jit(solution)/shard_map/all_gather | solution.py:80
  31.3 6.3 %convolution_bitcast_fusion = f32[3,4,512]{2,1,0:T(4,128)S(1)} fusion(bf16[3,4096,512]{2,1,0:T(8,128)(2,1)} %param.12, bf16[4,4096]{1,0:T(4,128)(2,1)S(1)} %all_gather.33), kind=kOutput, calls=%fused_computation.23 | convolution fusion | flops 50331648 | bytes 12640256 | tf_op jit(solution)/shard_map/tn,cnf->ctf/dot_general | solution.py:82
  37.8 0.5 multiply_cosine_fusion
  38.4 65.3 %all-gather.9.cloned.1.call-done = bf16[512,4096]{1,0:T(8,128)(2,1)} async-done(((bf16[512,512]{1,0:T(8,128)(2,1)}), bf16[512,4096]{1,0:T(8,128)(2,1)}) %all-gather.9.cloned.1.call-update) | async-done | bytes 4194320 | tf_op jit(solution)/shard_map/all_gather | solution.py:79
  103.7 10.6 %fusion.11 = f32[3,512,512]{1,2,0:T(8,128)S(1)} fusion(bf16[3,4096,512]{2,1,0:T(8,128)(2,1)} %param.12, bf16[512,4096]{1,0:T(8,128)(2,1)} %all-gather.9.cloned.1.call-done), kind=kOutput, calls=%fused_computation.21 | convolution fusion | flops 6442450944 | bytes 19922944 | tf_op jit(solution)/shard_map/tn,cnf->ctf/dot_general | solution.py:81
  114.3 1.7 copy-done.1
  116.0 0.4 multiply_reduce_fusion.2
  116.4 14.3 %all-reduce = (f32[512]{0:T(512)S(1)}, f32[512]{0:T(512)S(1)}, f32[4]{0:T(128)S(1)}, f32[4]{0:T(128)S(1)}) all-reduce(f32[512]{0:T(512)S(1)} %get-tuple-element.184, f32[512]{0:T(512)S(1)} %get-tuple-element.183, f32[4]{0:T(128)S(1)} %get-tuple-element.186, f32[4]{0:T(128)S(1)} %get-tuple-element.185), channel_id=1, replica_groups=mesh['seq'=16,'tp'=8] {'tp'}, use_global_device_ids=true, to_apply=%region_3.0 | all-reduce | flops 1032 | bytes 8256 | tf_op jit(solution)/shard_map/psum | solution.py:85
  132.2 1.1 pad_maximum_fusion
  133.3 1.3 slice.118
  134.8 1.1 copy.24
  136.5 0.6 broadcast_and_fusion
  137.5 1.4 fusion.29
  139.1 1.3 fusion.27
  140.4 29.3 %all-gather.2 = f32[64,4,128]{2,1,0:T(4,128)S(1)} all-gather(f32[4,4,128]{2,1,0:T(4,128)S(1)} %bitcast.96), channel_id=4, replica_groups=mesh['seq'=16,'tp'=8] {'seq'}, dimensions={0}, use_global_device_ids=true | all-gather | bytes 139264 | tf_op jit(solution)/shard_map/all_gather | solution.py:14
  170.6 19.6 %all-gather.4 = f32[16,4,4]{2,1,0:T(4,128)S(1)} all-gather(f32[1,4,4]{2,1,0:T(4,128)S(1)} %bitcast.99), channel_id=3, replica_groups=mesh['seq'=16,'tp'=8] {'seq'}, dimensions={0}, use_global_device_ids=true | all-gather | bytes 1088 | tf_op jit(solution)/shard_map/all_gather | solution.py:14
  190.1 20.8 %all-gather.3 = f32[16,4,4]{2,1,0:T(4,128)S(1)} all-gather(f32[1,4,4]{2,1,0:T(4,128)S(1)} %bitcast.97), channel_id=2, replica_groups=mesh['seq'=16,'tp'=8] {'seq'}, dimensions={0}, use_global_device_ids=true | all-gather | bytes 1088 | tf_op jit(solution)/shard_map/all_gather | solution.py:14
  211.0 13.4 %fusion.3 = (f32[4,4,128]{2,1,0:T(4,128)S(1)}, f32[4,4,128,2048]{3,2,1,0:T(8,128)}) fusion(pred[4,128,2048]{2,1,0:T(8,128)(4,1)S(1)} %broadcast_and_fusion, bf16[4,2048,4,128]{3,1,2,0:T(8,128)(2,1)} %all-gather.11.cloned.1.call-done, bf16[4,128,4,64]{3,1,2,0:T(8,128)(2,1)S(1)} %copy.21, bf16[4,128,4,64]{3,1,2,0:T(8,128)(2,1)S(1)} %copy.20), kind=kOutput, calls=%fused_computation.10 | convolution fusion | flops 1087371264 | bytes 26746880 | tf_op jit(solution)/shard_map/sphe,snhe->shpn/dot_general | solution.py:39
  224.3 8.4 %fusion.4 = f32[4,4,128]{2,1,0:T(4,128)S(1)} fusion(f32[4,4,128,2048]{3,2,1,0:T(8,128)} %get-tuple-element.235, f32[4,4,128]{2,1,0:T(4,128)S(1)} %broadcast_maximum_fusion, pred[4,128,2048]{2,1,0:T(8,128)(4,1)S(1)} %broadcast_and_fusion), kind=kLoop, calls=%fused_computation.11 | loop fusion | flops 20969472 | bytes 17842176 | tf_op jit(solution)/shard_map/reduce_sum | solution.py:50
  232.7 51.6 %all-gather.13.cloned.1.call-done = bf16[4,2048,4,128]{3,1,2,0:T(8,128)(2,1)} async-done(((bf16[4,128,4,128]{3,1,2,0:T(8,128)(2,1)}), bf16[4,2048,4,128]{3,1,2,0:T(8,128)(2,1)}) %all-gather.13.cloned.1.call-update) | async-done | bytes 8388624 | tf_op jit(solution)/shard_map/all_gather | solution.py:128
  284.4 11.7 %divide_convert_fusion = bf16[4,128,4,128]{3,1,2,0:T(8,128)(2,1)S(1)} fusion(bf16[4,2048,4,128]{3,1,2,0:T(8,128)(2,1)} %all-gather.13.cloned.1.call-done, f32[4,4,128,2048]{3,2,1,0:T(8,128)} %get-tuple-element.235, f32[4,4,128]{2,1,0:T(4,128)S(1)} %broadcast_maximum_fusion, pred[4,128,2048]{2,1,0:T(8,128)(4,1)S(1)} %broadcast_and_fusion, ...), kind=kOutput, calls=%fused_computation.26 | convolution fusion | flops 1095237632 | bytes 26755072 | tf_op jit(solution)/shard_map/shpn,snhe->shpe/dot_general | solution.py:51
  296.1 0.4 copy.25
  296.5 4.3 convolution_convert_fusion
  300.9 1.6 while.19
  302.8 2.8 convolution_convert_fusion.1
  305.6 28.8 %psum.47 = bf16[4,4096]{1,0:T(4,128)(2,1)S(1)} all-reduce(bf16[4,4096]{1,0:T(4,128)(2,1)S(1)} %convolution_convert_fusion.1), channel_id=1, replica_groups=mesh['seq'=16,'tp'=8] {'tp'}, use_global_device_ids=true, to_apply=%region_16.17 | all-reduce | flops 16384 | bytes 65536 | tf_op jit(solution)/shard_map/psum | solution.py:169
  334.6 0.7 add_convert_fusion.3
  335.3 146.6 %all-reduce.3.cloned.1.call-done = bf16[512,4096]{1,0:T(8,128)(2,1)} async-done(((bf16[512,4096]{1,0:T(8,128)(2,1)}), bf16[512,4096]{1,0:T(8,128)(2,1)}) %all-reduce.3.cloned.1.call-update) | async-done | bytes 4194320 | tf_op jit(solution)/shard_map/psum | solution.py:168
  481.9 3.1 multiply_reduce_fusion
  484.9 3.3 convert_element_type.95
  488.2 1.0 add_convert_fusion
  (98 shorter events, 5.9 us)
Async XLA Ops:
  7.2 96.5 %all-gather.9.cloned.1.call-start = ((), (), s32[]{:S(2)}) async-start(), calls=%async_computation | async-start | bytes 4718592 | tf_op jit(solution)/shard_map/all_gather | solution.py:79
  7.9 203.1 %all-gather.11.cloned.1.call-start = ((), (), s32[]{:S(2)}) async-start(), calls=%async_computation.1 | async-start | bytes 8912896 | tf_op jit(solution)/shard_map/all_gather | solution.py:127
  38.4 92.3 %copy-start.5 = (f32[512]{0:T(512)S(1)}, f32[512]{0:T(512)}, u32[]{:S(2)}) copy-start(f32[512]{0:T(512)} %param.15) | copy-start | bytes 6148
  38.4 92.5 %copy-start.6 = (f32[512]{0:T(512)S(1)}, f32[512]{0:T(512)}, u32[]{:S(2)}) copy-start(f32[512]{0:T(512)} %param.14) | copy-start | bytes 6148
  114.3 1.7 copy-start.1
  116.4 19.6 %copy-start.7 = (s32[4]{0:T(128)S(1)}, s32[4]{0:T(128)}, u32[]{:S(2)}) copy-start(s32[4]{0:T(128)} %param.17) | copy-start | bytes 52
  133.3 151.1 %all-gather.13.cloned.1.call-start = ((), (), s32[]{:S(2)}) async-start(), calls=%async_computation.2 | async-start | bytes 8912896 | tf_op jit(solution)/shard_map/all_gather | solution.py:128
  135.9 346.0 %all-reduce.3.cloned.1.call-start = ((), (), s32[]{:S(2)}) async-start(), calls=%async_computation.3 | async-start | bytes 8388608 | tf_op jit(solution)/shard_map/psum | solution.py:168
  284.4 12.1 %copy-start = (bf16[512,4096]{1,0:T(8,128)(2,1)S(1)}, bf16[512,4096]{1,0:T(8,128)(2,1)}, u32[]{:S(2)}) copy-start(bf16[512,4096]{1,0:T(8,128)(2,1)} %param.13) | copy-start | bytes 12582916
  296.5 38.1 %copy-start.3 = (bf16[4,512]{1,0:T(4,128)(2,1)S(1)}, bf16[4,512]{1,0:T(4,128)(2,1)}, u32[]{:S(2)}) copy-start(bf16[4,512]{1,0:T(4,128)(2,1)} %param.11) | copy-start | bytes 12292
  296.5 38.1 %copy-start.4 = (f32[512]{0:T(512)S(1)}, f32[512]{0:T(512)}, u32[]{:S(2)}) copy-start(f32[512]{0:T(512)} %param.16) | copy-start | bytes 6148
  335.3 152.9 %copy-start.2 = (bf16[4,128,512]{2,1,0:T(8,128)(2,1)S(1)}, bf16[4,128,512]{2,1,0:T(8,128)(2,1)}, u32[]{:S(2)}) copy-start(bf16[4,128,512]{2,1,0:T(8,128)(2,1)} %param.10) | copy-start | bytes 1572868
Sparse Core Ops, SparseCore 0:
  9.6 93.9 all-gather.8
  133.4 77.0 all-gather.10
  213.6 70.7 all-gather.12
  301.0 180.8 all-reduce.2
where the time goes:
time: 496 us
  waiting for transfers between devices  264 us (53%)
  blocking collectives  136 us (27%)
  matrix products  51.9 us (10%)
  other arithmetic  23 us (5%)
  between operations  14.1 us (3%)
  local copies, waits for them, and re-layouts  6.25 us (1%)
    psum x1, waiting for transfers between devices, body(): lax.psum(part_rows.astype(jnp.bfloat16), 'tp').astype(jnp.float32)  147 us
    all_gather x3, blocking collectives, joined(): everything = jax.tree.map(lambda part: lax.all_gather(part, axis), value)  69.7 us
    all_gather x1, waiting for transfers between devices, body(): row_piece = lax.all_gather(flat_rows, 'tp', axis=1, tiled=True)  65.3 us
    all_gather x1, waiting for transfers between devices, body(): lax.all_gather(values, 'seq', axis=1, tiled=True)  51.6 us
    psum x1, blocking collectives, body(): lax.psum(part_new.astype(jnp.bfloat16), 'tp').astype(jnp.float32)  28.8 us
    all_gather x1, blocking collectives, body(): new_piece = lax.all_gather(new_tokens, 'tp', axis=1, tiled=True)  23.3 us
    psum x1, blocking collectives, body(): lax.psum((jnp.sum(query_rows * query_rows, -1), jnp.sum(key_rows * key_ro...  14.3 us
    dot_general x1, matrix products, fold_step(): jnp.einsum('sphe,snhe->shpn', queries, key_piece, preferred_element_type=...  13.4 us
  transfers between devices with their start and end apart: 4, of which 3 were waited for; matrix products, arithmetic and copies ran while one was open for 8% of the time, Pallas kernels for 0%

commit v1 on v0

--- a/solution.py
+++ b/solution.py
@@ -8,6 +8,12 @@
 rope_base = 500000.0
 norm_eps = 1e-06
 masked_fill = -1e30
+
+
+def summed_here(x, axis):
+    shards = lax.all_gather(x, axis, axis=0, tiled=False)
+    result = shards.sum(axis=0)
+    return result
 
 
 def joined(value, axis, combine):
@@ -165,7 +171,7 @@
     part_rows = jnp.dot(attention, w_out, preferred_element_type=jnp.float32)
     part_new = jnp.dot(new_attention, w_out, preferred_element_type=jnp.float32)
     sum_rows, sum_new = (
-        lax.psum(part_rows.astype(jnp.bfloat16), "tp").astype(jnp.float32),
+        summed_here(part_rows.astype(jnp.bfloat16), "tp").astype(jnp.float32),
         lax.psum(part_new.astype(jnp.bfloat16), "tp").astype(jnp.float32),
     )
     mean_rows = jnp.mean(sum_rows * sum_rows, -1)

time: 496 us -> 968 us (1.95)
  waiting for transfers between devices: 264 us -> 732 us
  other arithmetic: 23 us -> 37.2 us
    all_gather x0 -> x1, waiting for transfers between devices: none -> 542 us  [summed_here(): shards = lax.all_gather(x, axis, axis=0, tiled=False)]
    psum x1 -> x0, waiting for transfers between devices: 147 us -> none  [body(): lax.psum(part_rows.astype(jnp.bfloat16), 'tp').astype(jnp.float32)]
    all_gather x1, waiting for transfers between devices: 0.01 us -> 72 us  [body(): lax.all_gather(keys, 'seq', axis=1, tiled=True)]
    reduce_sum x0 -> x1, other arithmetic: none -> 14.2 us  [summed_here(): result = shards.sum(axis=0)]
  transfers between devices with their start and end apart: 4 -> 4, of which waited for: 3 -> 4; matrix products, arithmetic and copies ran while one was open for 8% -> 4% of each run, Pallas kernels for 0% -> 0%
where the time goes in v1:
time: 968 us
  waiting for transfers between devices  732 us (76%)
  blocking collectives  128 us (13%)
  matrix products  49.9 us (5%)
  other arithmetic  37.2 us (4%)
  between operations  14.1 us (1%)
    all_gather x1, waiting for transfers between devices, summed_here(): shards = lax.all_gather(x, axis, axis=0, tiled=False)  542 us
    all_gather x1, waiting for transfers between devices, body(): lax.all_gather(keys, 'seq', axis=1, tiled=True)  72 us
    all_gather x1, waiting for transfers between devices, body(): row_piece = lax.all_gather(flat_rows, 'tp', axis=1, tiled=True)  65.3 us
    all_gather x3, blocking collectives, joined(): everything = jax.tree.map(lambda part: lax.all_gather(part, axis), value)  60.7 us
    all_gather x1, waiting for transfers between devices, body(): lax.all_gather(values, 'seq', axis=1, tiled=True)  52.2 us
    psum x1, blocking collectives, body(): lax.psum(part_new.astype(jnp.bfloat16), 'tp').astype(jnp.float32)  29.6 us
    all_gather x1, blocking collectives, body(): new_piece = lax.all_gather(new_tokens, 'tp', axis=1, tiled=True)  23.3 us
  transfers between devices with their start and end apart: 4, of which 4 were waited for; matrix products, arithmetic and copies ran while one was open for 4% of the time, Pallas kernels for 0%

profile of v1, /device:TPU:1, one launch (start us, length us, event | category | flops | bytes accessed | tf_op | source)
XLA Modules:
  0.0 968.1 jit_solution(16050541007025410287)
XLA Ops:
  7.2 0.7 all-gather.11.cloned.1.call-update
  7.9 23.3 %all_gather.41 = bf16[4,4096]{1,0:T(4,128)(2,1)S(1)} all-gather(bf16[4,512]{1,0:T(4,128)(2,1)} %param.11), channel_id=1, replica_groups=mesh['seq'=16,'tp'=8] {'tp'}, dimensions={1}, use_global_device_ids=true | all-gather | bytes 36864 | tf_op jit(solution)/shard_map/all_gather | solution.py:86
  31.3 6.3 convolution_bitcast_fusion
  37.8 0.5 multiply_cosine_fusion
  38.4 65.3 %all-gather.11.cloned.1.call-done = bf16[512,4096]{1,0:T(8,128)(2,1)} async-done(((bf16[512,512]{1,0:T(8,128)(2,1)}), bf16[512,4096]{1,0:T(8,128)(2,1)}) %all-gather.11.cloned.1.call-update) | async-done | bytes 4194320 | tf_op jit(solution)/shard_map/all_gather | solution.py:85
  103.7 10.6 %fusion.11 = f32[3,512,512]{1,2,0:T(8,128)S(1)} fusion(bf16[3,4096,512]{2,1,0:T(8,128)(2,1)} %param.12, bf16[512,4096]{1,0:T(8,128)(2,1)} %all-gather.11.cloned.1.call-done), kind=kOutput, calls=%fused_computation.21 | convolution fusion | flops 6442450944 | bytes 19922944 | tf_op jit(solution)/shard_map/tn,cnf->ctf/dot_general | solution.py:87
  114.3 1.7 copy-done.3
  116.0 0.4 multiply_reduce_fusion.2
  116.4 14.3 %all-reduce = (f32[512]{0:T(512)S(1)}, f32[512]{0:T(512)S(1)}, f32[4]{0:T(128)S(1)}, f32[4]{0:T(128)S(1)}) all-reduce(f32[512]{0:T(512)S(1)} %get-tuple-element.184, f32[512]{0:T(512)S(1)} %get-tuple-element.183, f32[4]{0:T(128)S(1)} %get-tuple-element.186, f32[4]{0:T(128)S(1)} %get-tuple-element.185), channel_id=1, replica_groups=mesh['seq'=16,'tp'=8] {'tp'}, use_global_device_ids=true, to_apply=%region_3.0 | all-reduce | flops 1032 | bytes 8256 | tf_op jit(solution)/shard_map/psum | solution.py:91
  132.2 1.1 pad_maximum_fusion
  133.3 1.3 slice.118
  134.8 1.1 copy.24
  136.5 0.6 broadcast_and_fusion
  137.9 72.0 %all-gather.13.cloned.1.call-done = bf16[4,2048,4,128]{3,1,2,0:T(8,128)(2,1)} async-done(((bf16[4,128,4,128]{3,1,2,0:T(8,128)(2,1)}), bf16[4,2048,4,128]{3,1,2,0:T(8,128)(2,1)}) %all-gather.13.cloned.1.call-update) | async-done | bytes 8388624 | tf_op jit(solution)/shard_map/all_gather | solution.py:133
  209.9 13.4 %fusion.3 = (f32[4,4,128]{2,1,0:T(4,128)S(1)}, f32[4,4,128,2048]{3,2,1,0:T(8,128)}) fusion(pred[4,128,2048]{2,1,0:T(8,128)(4,1)S(1)} %broadcast_and_fusion, bf16[4,2048,4,128]{3,1,2,0:T(8,128)(2,1)} %all-gather.13.cloned.1.call-done, bf16[4,128,4,64]{3,1,2,0:T(8,128)(2,1)S(1)} %copy.21, bf16[4,128,4,64]{3,1,2,0:T(8,128)(2,1)S(1)} %copy.20), kind=kOutput, calls=%fused_computation.10 | convolution fusion | flops 1087371264 | bytes 26746880 | tf_op jit(solution)/shard_map/sphe,snhe->shpn/dot_general | solution.py:45
  223.2 8.4 fusion.4
  231.6 52.2 %all-gather.15.cloned.1.call-done = bf16[4,2048,4,128]{3,1,2,0:T(8,128)(2,1)} async-done(((bf16[4,128,4,128]{3,1,2,0:T(8,128)(2,1)}), bf16[4,2048,4,128]{3,1,2,0:T(8,128)(2,1)}) %all-gather.15.cloned.1.call-update) | async-done | bytes 8388624 | tf_op jit(solution)/shard_map/all_gather | solution.py:134
  283.8 11.7 %divide_convert_fusion = bf16[4,128,4,128]{3,1,2,0:T(8,128)(2,1)S(1)} fusion(bf16[4,2048,4,128]{3,1,2,0:T(8,128)(2,1)} %all-gather.15.cloned.1.call-done, f32[4,4,128,2048]{3,2,1,0:T(8,128)} %get-tuple-element.235, f32[4,4,128]{2,1,0:T(4,128)S(1)} %broadcast_maximum_fusion, pred[4,128,2048]{2,1,0:T(8,128)(4,1)S(1)} %broadcast_and_fusion, ...), kind=kOutput, calls=%fused_computation.26 | convolution fusion | flops 1095237632 | bytes 26755072 | tf_op jit(solution)/shard_map/shpn,snhe->shpe/dot_general | solution.py:57
  295.6 0.4 copy.25
  296.0 4.4 convolution_convert_fusion
  301.9 20.6 %all-gather.3 = f32[64,4,128]{2,1,0:T(4,128)S(1)} all-gather(f32[4,4,128]{2,1,0:T(4,128)S(1)} %bitcast.98), channel_id=5, replica_groups=mesh['seq'=16,'tp'=8] {'seq'}, dimensions={0}, use_global_device_ids=true | all-gather | bytes 139264 | tf_op jit(solution)/shard_map/all_gather | solution.py:20
  322.6 20.3 %all-gather.4 = f32[16,4,4]{2,1,0:T(4,128)S(1)} all-gather(f32[1,4,4]{2,1,0:T(4,128)S(1)} %bitcast.99), channel_id=3, replica_groups=mesh['seq'=16,'tp'=8] {'seq'}, dimensions={0}, use_global_device_ids=true | all-gather | bytes 1088 | tf_op jit(solution)/shard_map/all_gather | solution.py:20
  342.8 19.8 %all-gather.5 = f32[16,4,4]{2,1,0:T(4,128)S(1)} all-gather(f32[1,4,4]{2,1,0:T(4,128)S(1)} %bitcast.101), channel_id=4, replica_groups=mesh['seq'=16,'tp'=8] {'seq'}, dimensions={0}, use_global_device_ids=true | all-gather | bytes 1088 | tf_op jit(solution)/shard_map/all_gather | solution.py:20
  362.8 1.6 while.19
  364.5 2.8 convolution_convert_fusion.1
  367.4 29.6 %psum.39 = bf16[4,4096]{1,0:T(4,128)(2,1)S(1)} all-reduce(bf16[4,4096]{1,0:T(4,128)(2,1)S(1)} %convolution_convert_fusion.1), channel_id=1, replica_groups=mesh['seq'=16,'tp'=8] {'tp'}, use_global_device_ids=true, to_apply=%region_16.17 | all-reduce | flops 16384 | bytes 65536 | tf_op jit(solution)/shard_map/psum | solution.py:175
  397.1 0.7 add_convert_fusion.3
  397.8 542.2 %all-gather.17.cloned.1.call-done = bf16[4096,4096]{1,0:T(8,128)(2,1)} async-done(((bf16[512,4096]{1,0:T(8,128)(2,1)}), bf16[4096,4096]{1,0:T(8,128)(2,1)}) %all-gather.17.cloned.1.call-update) | async-done | bytes 33554448 | tf_op jit(solution)/shard_map/all_gather | solution.py:14
  939.9 14.2 %reduce_sum.87 = bf16[512,4096]{1,0:T(8,128)(2,1)} reduce(bf16[8,512,4096]{2,1,0:T(8,128)(2,1)} %bitcast.89, bf16[]{:T(256)} %constant.82.clone.1), dimensions={0}, to_apply=%region_6.0 | reduce | flops 14680064 | bytes 37748736 | tf_op jit(solution)/shard_map/reduce_sum | solution.py:15
  954.1 3.1 multiply_reduce_fusion
  957.2 3.3 convert_element_type.97
  960.5 1.0 add_convert_fusion
  (103 shorter events, 6.7 us)
Async XLA Ops:
  7.2 96.5 %all-gather.11.cloned.1.call-start = ((), (), s32[]{:S(2)}) async-start(), calls=%async_computation | async-start | bytes 4718592 | tf_op jit(solution)/shard_map/all_gather | solution.py:85
  7.9 202.0 %all-gather.13.cloned.1.call-start = ((), (), s32[]{:S(2)}) async-start(), calls=%async_computation.1 | async-start | bytes 8912896 | tf_op jit(solution)/shard_map/all_gather | solution.py:133
  38.4 92.3 %copy-start.7 = (f32[512]{0:T(512)S(1)}, f32[512]{0:T(512)}, u32[]{:S(2)}) copy-start(f32[512]{0:T(512)} %param.15) | copy-start | bytes 6148
  38.4 92.5 %copy-start.8 = (f32[512]{0:T(512)S(1)}, f32[512]{0:T(512)}, u32[]{:S(2)}) copy-start(f32[512]{0:T(512)} %param.14) | copy-start | bytes 6148
  114.3 1.7 copy-start.3
  116.4 19.8 %copy-start.9 = (s32[4]{0:T(128)S(1)}, s32[4]{0:T(128)}, u32[]{:S(2)}) copy-start(s32[4]{0:T(128)} %param.17) | copy-start | bytes 52
  133.3 150.5 %all-gather.15.cloned.1.call-start = ((), (), s32[]{:S(2)}) async-start(), calls=%async_computation.2 | async-start | bytes 8912896 | tf_op jit(solution)/shard_map/all_gather | solution.py:134
  135.9 804.0 %all-gather.17.cloned.1.call-start = ((), (), s32[]{:S(2)}) async-start(), calls=%async_computation.3 | async-start | bytes 37748736 | tf_op jit(solution)/shard_map/all_gather | solution.py:14
  283.8 12.1 %copy-start.2 = (bf16[512,4096]{1,0:T(8,128)(2,1)S(1)}, bf16[512,4096]{1,0:T(8,128)(2,1)}, u32[]{:S(2)}) copy-start(bf16[512,4096]{1,0:T(8,128)(2,1)} %param.13) | copy-start | bytes 12582916
  296.0 5.1 copy-start
  296.0 5.7 copy-start.1
  296.0 101.1 %copy-start.5 = (bf16[4,512]{1,0:T(4,128)(2,1)S(1)}, bf16[4,512]{1,0:T(4,128)(2,1)}, u32[]{:S(2)}) copy-start(bf16[4,512]{1,0:T(4,128)(2,1)} %param.11) | copy-start | bytes 12292
  296.0 101.1 %copy-start.6 = (f32[512]{0:T(512)S(1)}, f32[512]{0:T(512)}, u32[]{:S(2)}) copy-start(f32[512]{0:T(512)} %param.16) | copy-start | bytes 6148
  954.1 6.4 copy-start.4
Sparse Core Ops, SparseCore 0:
  9.6 93.9 all-gather.10
  133.4 76.3 all-gather.12
  213.0 70.8 all-gather.14
  300.6 639.2 all-gather.16
